TPU v7x, 512 devices: a whole 4x4x16 slice. The times are simulated.
512 devices in a mesh: row: 32 (over z, core), col: 16 (over y, x).
Axes of the slice: x: 4, y: 4, z: 16, core: 2. Of those that a mesh axis runs over, the one named last changes fastest.
Arguments:
- inv_top: float32 [2, 4096, 4096], P(None, 'row', 'col'), may hold values from -0.0625 to 0.0625
- inv_bottom: float32 [2, 4096, 4096], P(None, 'row', 'col'), may hold values from -0.0625 to 0.0625
- lower_panel: float32 [2, 4096, 4096], P(None, 'row', 'col'), may hold values from -0.0625 to 0.0625
- rhs_top: float32 [2, 4096, 128], P(None, 'col'), may hold values from -6 to 6
- rhs_bottom: float32 [2, 4096, 128], P(None, 'row'), may hold values from -6 to 6
- source_xy: float32 [2, 2, 4096], P(None, None, 'col'), may hold values from -20 to 20
- source_depth: float32 [2, 4096], P(None, 'col'), may hold values from -2 to -0.5
- body_label: int32 [2, 4096], P(None, 'col'), may hold values 0 or 1
- field_xy: float32 [2, 98304], P(None, 'row'), may hold values from -20 to 20
- region_label: int32 [98304], P('row'), may hold values 0 or 1
- lid_table: float32 [2, 2], replicated, may hold values from 0.3 to 3
- wave_number: float32 [1], replicated, may hold values from 0.5 to 1.5
Outputs:
- strengths: float32 [2, 2, 4096, 128], P(None, None, 'col')
- elevation: float32 [98304, 2, 128], P(('row', 'col'))
All inputs are finite; a program needn't handle non-finite values. No bound on the sum of `body_label` or of `region_label` on one device may be relied on, other than what follows from the above.
Results may differ from a plain program's by a relative error of at most 0.004.
Values sent between devices are 32-bit elements; how exact they have to be, the bound alone decides.
No kernel may reach another device: no remote copies, remote signals or barrier semaphores. Data moves between devices by JAX's collectives and lax.ppermute only.
A program may use at most 64 MiB of HBM per device.

v0:
```python
import jax
import jax.numpy as jnp
from jax import lax
from jax.sharding import PartitionSpec as P


def complex_product(matrix, vector):
    highest = lax.Precision.HIGHEST
    real_part = jnp.dot(
        matrix[0], vector[0], precision=highest, preferred_element_type=jnp.float32
    ) - jnp.dot(matrix[1], vector[1], precision=highest, preferred_element_type=jnp.float32)
    imag_part = jnp.dot(
        matrix[0], vector[1], precision=highest, preferred_element_type=jnp.float32
    ) + jnp.dot(matrix[1], vector[0], precision=highest, preferred_element_type=jnp.float32)
    return jnp.stack([real_part, imag_part])


def green_tile(
    point_x, point_y, region, source_x, source_y, src_depth, src_label, lid_table, wave_value
):
    delta_x = point_x[:, None] - source_x[None, :]
    delta_y = point_y[:, None] - source_y[None, :]
    distance = jnp.sqrt(delta_x * delta_x + delta_y * delta_y + (src_depth * src_depth)[None, :])
    lid_first = jnp.where(region == 1, lid_table[1, 0], lid_table[0, 0])
    lid_second = jnp.where(region == 1, lid_table[1, 1], lid_table[0, 1])
    factor = jnp.where(src_label[None, :] == 1, lid_second[:, None], lid_first[:, None])
    amplitude = factor * jnp.exp(wave_value * src_depth)[None, :] / distance
    phase_angle = wave_value * distance
    return (
        (amplitude * jnp.cos(phase_angle)).astype(jnp.bfloat16),
        (amplitude * jnp.sin(phase_angle)).astype(jnp.bfloat16),
    )


def per_device(
    inv_top,
    inv_bottom,
    lower_panel,
    rhs_top,
    rhs_bottom,
    source_xy,
    source_depth,
    body_label,
    field_xy,
    region_label,
    lid_table,
    wave_number,
):
    col_rows = rhs_top.shape[1]

    def to_columns(row_block):
        gathered = lax.all_gather(row_block, "row", axis=1, tiled=True)
        return lax.dynamic_slice_in_dim(gathered, lax.axis_index("col") * col_rows, col_rows, 1)

    def column_total(partial_sum):
        return lax.psum(partial_sum, "col")

    top_solved = to_columns(column_total(complex_product(inv_top, rhs_top)))
    remainder = rhs_bottom - column_total(complex_product(lower_panel, top_solved))
    bottom_solved = to_columns(column_total(complex_product(inv_bottom, to_columns(remainder))))
    strengths = jnp.stack([top_solved, bottom_solved])
    weights = strengths.astype(jnp.bfloat16)
    right_count = weights.shape[3]
    src_real = weights[:, 0].reshape(-1, right_count)
    src_imag = weights[:, 1].reshape(-1, right_count)
    source_x = source_xy[0].reshape(-1)
    source_y = source_xy[1].reshape(-1)
    src_depth = source_depth.reshape(-1)
    src_label = body_label.reshape(-1)
    wave_value = wave_number[0]
    out_rows = field_xy.shape[1] // lax.axis_size("col")

    def block_term(first_row, block_rows):
        point_x = lax.dynamic_slice_in_dim(field_xy[0], first_row, block_rows)
        point_y = lax.dynamic_slice_in_dim(field_xy[1], first_row, block_rows)
        region = lax.dynamic_slice_in_dim(region_label, first_row, block_rows)
        tile_real, tile_imag = green_tile(
            point_x,
            point_y,
            region,
            source_x,
            source_y,
            src_depth,
            src_label,
            lid_table,
            wave_value,
        )
        real_part = jnp.dot(tile_real, src_real, preferred_element_type=jnp.float32) - jnp.dot(
            tile_imag, src_imag, preferred_element_type=jnp.float32
        )
        imag_part = jnp.dot(tile_real, src_imag, preferred_element_type=jnp.float32) + jnp.dot(
            tile_imag, src_real, preferred_element_type=jnp.float32
        )
        return jnp.stack([real_part, imag_part], axis=1)

    unit_count = out_rows * lax.axis_size("col") // out_rows
    group_units = max(
        (
            divisor
            for divisor in range(1, unit_count + 1)
            if unit_count % divisor == 0 and divisor * out_rows <= max(512, out_rows)
        )
    )
    block_rows = group_units * out_rows
    steps_count = out_rows * lax.axis_size("col") // block_rows

    def one_block(block_index):
        return block_term(block_index * block_rows, block_rows)

    results = lax.map(one_block, jnp.arange(steps_count, dtype=jnp.int32))
    elevation = lax.psum_scatter(
        results.reshape(out_rows * lax.axis_size("col"), 2, right_count),
        "col",
        scatter_dimension=0,
        tiled=True,
    )
    return (strengths, elevation)


def solution(mesh):
    in_specs = (
        P(None, "row", "col"),
        P(None, "row", "col"),
        P(None, "row", "col"),
        P(None, "col", None),
        P(None, "row", None),
        P(None, None, "col"),
        P(None, "col"),
        P(None, "col"),
        P(None, "row"),
        P("row"),
        P(),
        P(),
    )
    out_specs = (P(None, None, "col", None), P(("row", "col"), None, None))
    return jax.shard_map(
        per_device, mesh=mesh, in_specs=in_specs, out_specs=out_specs, check_vma=False
    )
```

profile of v0, /device:TPU:1, one launch (start us, length us, event | category | flops | bytes accessed | tf_op | source)
XLA Modules:
  0.0 916.5 jit_solution(3563913874649831330)
XLA Ops:
  13.0 117.3 %all-reduce.6.cloned.1.call-done = f32[2,128,128]{2,1,0:T(8,128)} async-done(((f32[2,128,128]{2,1,0:T(8,128)}), f32[2,128,128]{2,1,0:T(8,128)}) %all-reduce.6.cloned.1.call-update) | async-done | bytes 131088 | tf_op jit(solution)/shard_map/psum | solution.py:56
  130.4 77.4 %all-gather.4.cloned.1.call-done = f32[2,4096,128]{2,1,0:T(8,128)} async-done(((f32[2,128,128]{2,1,0:T(8,128)}), f32[2,4096,128]{2,1,0:T(8,128)}) %all-gather.4.cloned.1.call-update) | async-done | bytes 4194320 | tf_op jit(solution)/shard_map/all_gather | solution.py:52
  215.0 107.6 %all-reduce.8.cloned.1.call-done = f32[2,128,128]{1,2,0:T(8,128)} async-done(((f32[2,128,128]{1,2,0:T(8,128)}), f32[2,128,128]{1,2,0:T(8,128)}) %all-reduce.8.cloned.1.call-update) | async-done | bytes 131088 | tf_op jit(solution)/shard_map/psum | solution.py:56
  324.2 83.4 %all-gather.6.cloned.1.call-done = f32[2,4096,128]{1,2,0:T(8,128)} async-done(((f32[2,128,128]{1,2,0:T(8,128)}), f32[2,4096,128]{1,2,0:T(8,128)}) %all-gather.6.cloned.1.call-update) | async-done | bytes 4194320 | tf_op jit(solution)/shard_map/all_gather | solution.py:52
  413.1 107.1 %all-reduce.10.cloned.1.call-done = f32[2,128,128]{1,2,0:T(8,128)} async-done(((f32[2,128,128]{1,2,0:T(8,128)}), f32[2,128,128]{1,2,0:T(8,128)}) %all-reduce.10.cloned.1.call-update) | async-done | bytes 131088 | tf_op jit(solution)/shard_map/psum | solution.py:56
  521.3 83.3 %all-gather.8.cloned.1.call-done = f32[2,4096,128]{1,2,0:T(8,128)} async-done(((f32[2,128,128]{1,2,0:T(8,128)}), f32[2,4096,128]{1,2,0:T(8,128)}) %all-gather.8.cloned.1.call-update) | async-done | bytes 4194320 | tf_op jit(solution)/shard_map/all_gather | solution.py:52
  606.6 180.2 %while.11 = (s32[]{:T(128)}, f32[8,384,2,128]{3,2,1,0:T(2,128)}, s32[2,256]{1,0:T(2,128)S(1)}, s32[8]{0:T(128)S(1)}, s32[3072]{0:T(1024)}, /*index=5*/f32[2,2]{1...) while((s32[]{:T(128)}, f32[8,384,2,128]{3,2,1,0:T(2,128)}, ...), condition=%wide.region_4.5_spmd, body=%wide.region_3.4_spmd.sunk | while | flops 210962560 | bytes 3413047 | solution.py:110
  616.4 3.9 fusion.86
  620.4 3.9 fusion.83
  624.2 3.9 fusion.84
  638.9 3.9 fusion.86
  642.9 3.9 fusion.83
  646.7 3.9 fusion.84
  661.5 3.9 fusion.86
  665.4 3.9 fusion.83
  669.3 3.9 fusion.84
  683.9 3.9 fusion.86
  687.9 3.9 fusion.83
  691.7 3.9 fusion.84
  706.5 3.9 fusion.86
  710.4 3.9 fusion.83
  714.3 3.9 fusion.84
  728.9 3.9 fusion.86
  732.9 3.9 fusion.83
  736.7 3.9 fusion.84
  751.5 3.9 fusion.86
  755.4 3.9 fusion.83
  759.2 3.9 fusion.84
  773.9 3.9 fusion.86
  777.9 3.9 fusion.83
  781.7 3.9 fusion.84
  788.7 119.3 %all-reduce.12.cloned.1.call-done = f32[3072,2,128]{2,1,0:T(2,128)} async-done(((f32[3072,2,128]{2,1,0:T(2,128)}), f32[3072,2,128]{2,1,0:T(2,128)}) %all-reduce.12.cloned.1.call-update) | async-done | bytes 3145744
  (168 shorter events, 107.4 us)
Async XLA Ops:
  7.2 400.4 %copy-start = (f32[2,128,256]{2,1,0:T(8,128)S(1)}, f32[2,128,256]{2,1,0:T(8,128)}, u32[]{:S(2)}) copy-start(f32[2,128,256]{2,1,0:T(8,128)} %param.15) | copy-start | bytes 786436
  7.2 513.0 %copy-start.4 = (f32[2,256]{1,0:T(2,128)S(1)}, f32[2,256]{1,0:T(2,128)}, u32[]{:S(2)}) copy-start(f32[2,256]{1,0:T(2,128)} %param.20) | copy-start | bytes 6148
  7.2 513.1 %copy-start.5 = (f32[2,2,256]{2,1,0:T(2,128)S(1)}, f32[2,2,256]{2,1,0:T(2,128)}, u32[]{:S(2)}) copy-start(f32[2,2,256]{2,1,0:T(2,128)} %param.19) | copy-start | bytes 12292
  7.2 123.2 %all-reduce.6.cloned.1.call-start = ((), (), s32[]{:S(2)}) async-start(), calls=%async_computation | async-start | bytes 262144 | tf_op jit(solution)/shard_map/psum | solution.py:56
  12.9 593.6 %copy-start.1 = (f32[2,3072]{1,0:T(2,128)S(1)}, f32[2,3072]{1,0:T(2,128)}, u32[]{:S(2)}) copy-start(f32[2,3072]{1,0:T(2,128)} %param.22) | copy-start | bytes 73732
  12.9 593.6 %copy-start.2 = (f32[2,2]{1,0:T(2,128)S(1)}, f32[2,2]{1,0:T(2,128)}, u32[]{:S(2)}) copy-start(f32[2,2]{1,0:T(2,128)} %param.24) | copy-start | bytes 52
  12.9 593.6 %copy-start.3 = (s32[2,256]{1,0:T(2,128)S(1)}, s32[2,256]{1,0:T(2,128)}, u32[]{:S(2)}) copy-start(s32[2,256]{1,0:T(2,128)} %param.21) | copy-start | bytes 6148
  13.0 194.8 %all-gather.4.cloned.1.call-start = ((), (), s32[]{:S(2)}) async-start(), calls=%async_computation.1 | async-start | bytes 4325376 | tf_op jit(solution)/shard_map/all_gather | solution.py:52
  130.4 192.2 %all-reduce.8.cloned.1.call-start = ((), (), s32[]{:S(2)}) async-start(), calls=%async_computation.2 | async-start | bytes 262144 | tf_op jit(solution)/shard_map/psum | solution.py:56
  213.9 193.6 %all-gather.6.cloned.1.call-start = ((), (), s32[]{:S(2)}) async-start(), calls=%async_computation.3 | async-start | bytes 4325376 | tf_op jit(solution)/shard_map/all_gather | solution.py:52
  324.2 196.0 %all-reduce.10.cloned.1.call-start = ((), (), s32[]{:S(2)}) async-start(), calls=%async_computation.4 | async-start | bytes 262144 | tf_op jit(solution)/shard_map/psum | solution.py:56
  413.0 191.5 %all-gather.8.cloned.1.call-start = ((), (), s32[]{:S(2)}) async-start(), calls=%async_computation.5 | async-start | bytes 4325376 | tf_op jit(solution)/shard_map/all_gather | solution.py:52
  520.2 387.9 %all-reduce.12.cloned.1.call-start = ((), (), s32[]{:S(2)}) async-start(), calls=%async_computation.6 | async-start | bytes 6291456
Sparse Core Ops, SparseCore 0:
  13.1 117.2 all-reduce.5
  132.5 75.2 all-gather.3
  214.1 108.4 all-reduce.7
  325.0 82.4 all-gather.5
  413.1 106.9 all-reduce.9
  522.0 82.4 all-gather.7
  786.9 121.0 all-reduce.11
where the time goes:
time: 918 us; the launch traced here: 917 us
  waiting for transfers between devices  695 us (76%)
  matrix products  140 us (15%)
  other arithmetic  36.2 us (4%)
  local copies, waits for them, and re-layouts  24.9 us (3%)
  between operations  15 us (2%)
    psum x3, waiting for transfers between devices, column_total(): return lax.psum(partial_sum, 'col')  332 us
    all_gather x3, waiting for transfers between devices, to_columns(): gathered = lax.all_gather(row_block, 'row', axis=1, tiled=True)  244 us
    unnamed x8, waiting for transfers between devices  119 us
    dot_general x8, matrix products, block_term(): jnp.dot(tile_imag, src_imag, preferred_element_type=jnp.float32)  31.3 us
    dot_general x8, matrix products, block_term(): jnp.dot(tile_imag, src_real, preferred_element_type=jnp.float32)  31.3 us
    dot_general x8, matrix products, block_term(): jnp.dot(tile_real, src_imag, preferred_element_type=jnp.float32)  31 us
    dot_general x8, matrix products, block_term(): jnp.dot(tile_real, src_real, preferred_element_type=jnp.float32)  30.8 us
  transfers between devices with their start and end apart: 7, of which 7 were waited for; matrix products, arithmetic and copies ran while one was open for 0% of the time, Pallas kernels for 0%

commit v1 on v0

--- a/solution.py
+++ b/solution.py
@@ -2,6 +2,7 @@
 import jax.numpy as jnp
 from jax import lax
 from jax.sharding import PartitionSpec as P
+from jax.lax import all_gather
 
 
 def complex_product(matrix, vector):
@@ -53,7 +54,12 @@
         return lax.dynamic_slice_in_dim(gathered, lax.axis_index("col") * col_rows, col_rows, 1)
 
     def column_total(partial_sum):
-        return lax.psum(partial_sum, "col")
+
+        def _bring_rounds(slab_in):
+            f_now = jnp.sum(all_gather(slab_in, "col"), axis=0)
+            return f_now
+
+        return _bring_rounds(partial_sum)
 
     top_solved = to_columns(column_total(complex_product(inv_top, rhs_top)))
     remainder = rhs_bottom - column_total(complex_product(lower_panel, top_solved))

time: 918 us -> 759 us (0.83)
  waiting for transfers between devices: 695 us -> 531 us
    psum x3 -> x0, waiting for transfers between devices: 332 us -> none  [column_total(): return lax.psum(partial_sum, 'col')]
    all_gather x0 -> x3, waiting for transfers between devices: none -> 173 us  [_bring_rounds(): f_now = jnp.sum(all_gather(slab_in, 'col'), axis=0)]
where the time goes in v1:
time: 759 us; the launch traced here: 758 us
  waiting for transfers between devices  531 us (70%)
  matrix products  139 us (18%)
  other arithmetic  40.1 us (5%)
  local copies, waits for them, and re-layouts  26.1 us (3%)
  between operations  15.1 us (2%)
    all_gather x3, waiting for transfers between devices, to_columns(): gathered = lax.all_gather(row_block, 'row', axis=1, tiled=True)  239 us
    all_gather x3, waiting for transfers between devices, _bring_rounds(): f_now = jnp.sum(all_gather(slab_in, 'col'), axis=0)  173 us
    unnamed x8, waiting for transfers between devices  119 us
    dot_general x8, matrix products, block_term(): jnp.dot(tile_imag, src_imag, preferred_element_type=jnp.float32)  31.3 us
    dot_general x8, matrix products, block_term(): jnp.dot(tile_imag, src_real, preferred_element_type=jnp.float32)  31.3 us
    dot_general x8, matrix products, block_term(): jnp.dot(tile_real, src_imag, preferred_element_type=jnp.float32)  31 us
    dot_general x8, matrix products, block_term(): jnp.dot(tile_real, src_real, preferred_element_type=jnp.float32)  30.8 us
    select_n x8, other arithmetic, green_tile(): lid_second = jnp.where(region == 1, lid_table[1, 1], lid_table[0, 1])  15.7 us
  transfers between devices with their start and end apart: 7, of which 7 were waited for; matrix products, arithmetic and copies ran while one was open for 0% of the time, Pallas kernels for 0%

profile of v1, /device:TPU:1, one launch (start us, length us, event | category | flops | bytes accessed | tf_op | source)
XLA Modules:
  0.0 757.9 jit_solution(17576312427497108150)
XLA Ops:
  13.1 64.0 %all-gather.16.cloned.1.call-done = f32[32,128,128]{2,1,0:T(8,128)} async-done(((f32[2,128,128]{2,1,0:T(8,128)}), f32[32,128,128]{2,1,0:T(8,128)}) %all-gather.16.cloned.1.call-update) | async-done | bytes 2097168 | tf_op jit(solution)/shard_map/all_gather | solution.py:59
  79.5 75.2 %all-gather.10.cloned.1.call-done = f32[2,4096,128]{2,1,0:T(8,128)} async-done(((f32[2,128,128]{2,1,0:T(8,128)}), f32[2,4096,128]{2,1,0:T(8,128)}) %all-gather.10.cloned.1.call-update) | async-done | bytes 4194320 | tf_op jit(solution)/shard_map/all_gather | solution.py:53
  160.9 55.1 %all-gather.18.cloned.1.call-done = f32[32,128,128]{2,1,0:T(8,128)} async-done(((f32[2,128,128]{2,1,0:T(8,128)}), f32[32,128,128]{2,1,0:T(8,128)}) %all-gather.18.cloned.1.call-update) | async-done | bytes 2097168 | tf_op jit(solution)/shard_map/all_gather | solution.py:59
  218.7 82.3 %all-gather.12.cloned.1.call-done = f32[2,4096,128]{1,2,0:T(8,128)} async-done(((f32[2,128,128]{1,2,0:T(8,128)}), f32[2,4096,128]{1,2,0:T(8,128)}) %all-gather.12.cloned.1.call-update) | async-done | bytes 4194320 | tf_op jit(solution)/shard_map/all_gather | solution.py:53
  306.5 53.8 %all-gather.20.cloned.1.call-done = f32[32,128,128]{2,1,0:T(8,128)} async-done(((f32[2,128,128]{2,1,0:T(8,128)}), f32[32,128,128]{2,1,0:T(8,128)}) %all-gather.20.cloned.1.call-update) | async-done | bytes 2097168 | tf_op jit(solution)/shard_map/all_gather | solution.py:59
  363.9 81.2 %all-gather.14.cloned.1.call-done = f32[2,4096,128]{1,2,0:T(8,128)} async-done(((f32[2,128,128]{1,2,0:T(8,128)}), f32[2,4096,128]{1,2,0:T(8,128)}) %all-gather.14.cloned.1.call-update) | async-done | bytes 4194320 | tf_op jit(solution)/shard_map/all_gather | solution.py:53
  447.1 181.1 %while.11 = (s32[]{:T(128)}, f32[8,384,2,128]{3,2,1,0:T(2,128)}, s32[2,256]{1,0:T(2,128)S(1)}, s32[8]{0:T(128)S(1)}, s32[3072]{0:T(1024)}, /*index=5*/f32[2,2]{1...) while((s32[]{:T(128)}, f32[8,384,2,128]{3,2,1,0:T(2,128)}, ...), condition=%wide.region_4.5_spmd, body=%wide.region_3.4_spmd.sunk | while | flops 210962560 | bytes 3413047 | solution.py:116
  457.1 3.9 fusion.86
  461.0 3.9 fusion.83
  464.9 3.9 fusion.84
  479.7 3.9 fusion.86
  483.6 3.9 fusion.83
  487.5 3.9 fusion.84
  502.3 3.9 fusion.86
  506.2 3.9 fusion.83
  510.1 3.9 fusion.84
  524.9 3.9 fusion.86
  528.8 3.9 fusion.83
  532.7 3.9 fusion.84
  547.5 3.9 fusion.86
  551.4 3.9 fusion.83
  555.3 3.9 fusion.84
  570.1 3.9 fusion.86
  574.0 3.9 fusion.83
  577.9 3.9 fusion.84
  592.7 3.9 fusion.86
  596.7 3.9 fusion.83
  600.5 3.9 fusion.84
  615.3 3.9 fusion.86
  619.3 3.9 fusion.83
  623.1 3.9 fusion.84
  630.1 119.3 %all-reduce.3.cloned.1.call-done = f32[3072,2,128]{2,1,0:T(2,128)} async-done(((f32[3072,2,128]{2,1,0:T(2,128)}), f32[3072,2,128]{2,1,0:T(2,128)}) %all-reduce.3.cloned.1.call-update) | async-done | bytes 3145744
  (179 shorter events, 112.3 us)
Async XLA Ops:
  7.2 147.6 %copy-start = (f32[2,128,256]{2,1,0:T(8,128)S(1)}, f32[2,128,256]{2,1,0:T(8,128)}, u32[]{:S(2)}) copy-start(f32[2,128,256]{2,1,0:T(8,128)} %param.16) | copy-start | bytes 786436
  7.2 153.7 %copy-start.3 = (f32[2,128,128]{2,1,0:T(8,128)S(1)}, f32[2,128,128]{2,1,0:T(8,128)}, u32[]{:S(2)}) copy-start(f32[2,128,128]{2,1,0:T(8,128)} %param.18) | copy-start | bytes 393220
  7.2 69.9 %all-gather.16.cloned.1.call-start = ((), (), s32[]{:S(2)}) async-start(), calls=%async_computation.3 | async-start | bytes 2228224 | tf_op jit(solution)/shard_map/all_gather | solution.py:59
  11.0 289.9 %copy-start.1 = (f32[2,128,256]{2,1,0:T(8,128)S(1)}, f32[2,128,256]{2,1,0:T(8,128)}, u32[]{:S(2)}) copy-start(f32[2,128,256]{2,1,0:T(8,128)} %param.15) | copy-start | bytes 786436
  13.0 141.8 %all-gather.10.cloned.1.call-start = ((), (), s32[]{:S(2)}) async-start(), calls=%async_computation | async-start | bytes 4325376 | tf_op jit(solution)/shard_map/all_gather | solution.py:53
  79.5 136.6 %all-gather.18.cloned.1.call-start = ((), (), s32[]{:S(2)}) async-start(), calls=%async_computation.4 | async-start | bytes 2228224 | tf_op jit(solution)/shard_map/all_gather | solution.py:59
  160.0 202.9 %copy-start.6 = (f32[2,256]{1,0:T(2,128)S(1)}, f32[2,256]{1,0:T(2,128)}, u32[]{:S(2)}) copy-start(f32[2,256]{1,0:T(2,128)} %param.20) | copy-start | bytes 6148
  160.0 202.9 %copy-start.7 = (f32[2,2,256]{2,1,0:T(2,128)S(1)}, f32[2,2,256]{2,1,0:T(2,128)}, u32[]{:S(2)}) copy-start(f32[2,2,256]{2,1,0:T(2,128)} %param.19) | copy-start | bytes 12292
  160.8 140.1 %all-gather.12.cloned.1.call-start = ((), (), s32[]{:S(2)}) async-start(), calls=%async_computation.1 | async-start | bytes 4325376 | tf_op jit(solution)/shard_map/all_gather | solution.py:53
  218.6 228.5 %copy-start.2 = (f32[2,3072]{1,0:T(2,128)S(1)}, f32[2,3072]{1,0:T(2,128)}, u32[]{:S(2)}) copy-start(f32[2,3072]{1,0:T(2,128)} %param.22) | copy-start | bytes 73732
  218.6 228.5 %copy-start.4 = (f32[2,2]{1,0:T(2,128)S(1)}, f32[2,2]{1,0:T(2,128)}, u32[]{:S(2)}) copy-start(f32[2,2]{1,0:T(2,128)} %param.24) | copy-start | bytes 52
  218.6 228.5 %copy-start.5 = (s32[2,256]{1,0:T(2,128)S(1)}, s32[2,256]{1,0:T(2,128)}, u32[]{:S(2)}) copy-start(s32[2,256]{1,0:T(2,128)} %param.21) | copy-start | bytes 6148
  218.6 141.7 %all-gather.20.cloned.1.call-start = ((), (), s32[]{:S(2)}) async-start(), calls=%async_computation.5 | async-start | bytes 2228224 | tf_op jit(solution)/shard_map/all_gather | solution.py:59
  306.5 138.6 %all-gather.14.cloned.1.call-start = ((), (), s32[]{:S(2)}) async-start(), calls=%async_computation.2 | async-start | bytes 4325376 | tf_op jit(solution)/shard_map/all_gather | solution.py:53
  362.8 386.7 %all-reduce.3.cloned.1.call-start = ((), (), s32[]{:S(2)}) async-start(), calls=%async_computation.6 | async-start | bytes 6291456
Sparse Core Ops, SparseCore 0:
  13.1 63.9 all-gather.15
  79.8 74.9 all-gather.9
  160.9 55.1 all-gather.17
  218.7 82.1 all-gather.11
  306.6 53.6 all-gather.19
  362.9 82.1 all-gather.13
  628.3 121.0 all-reduce.2
